TPU v7x, 128 devices: a whole 4x4x4 slice. The times are simulated.
128 devices in a mesh: xb: 16 (over y, z), yb: 8 (over x, core).
Axes of the slice: x: 4, y: 4, z: 4, core: 2. Of those that a mesh axis runs over, the one named last changes fastest.
Arguments:
- initial_guess: float32 [128, 512, 256], P('xb', 'yb'), may hold values from -4 to 4
- right_side: float32 [128, 512, 256], P('xb', 'yb'), may hold values from -8 to 8
- coefficient: float32 [128, 512, 256], P('xb', 'yb'), may hold values from 0.3 to 3
Outputs:
- fine_field: float32 [128, 512, 256], P('xb', 'yb')
- middle_field: float32 [64, 256, 128], P('xb', 'yb')
- lower_field: float32 [32, 128, 64], P('xb', 'yb')
- coarse_field: float32 [16, 64, 32], P('xb', 'yb')
All inputs are finite; a program needn't handle non-finite values.
Results may differ from a plain program's by a relative error of at most 0.00002.
Values sent between devices are 32-bit elements; how exact they have to be, the bound alone decides.
No kernel may reach another device: no remote copies, remote signals or barrier semaphores. Data moves between devices by JAX's collectives and lax.ppermute only.
A program may use at most 192 MiB of HBM per device.

v0:
```python
import jax
import jax.numpy as jnp
from jax import lax
from jax.sharding import PartitionSpec as P

COARSE_ITERS = 8
damping_alpha = 0.05
cheb_theta = 1.15
cheb_delta = 0.85
cheb_sigma = cheb_theta / cheb_delta
cheb_first = 1.0 / cheb_sigma
cheb_second = 1.0 / (2.0 * cheb_sigma - cheb_first)
cheb_carry = cheb_second * cheb_first
cheb_resid = 2.0 * cheb_second / cheb_delta
jacobi_weight = 0.8


def exchange(items, axis, dim, forwards=()):
    count = lax.axis_size(axis)
    low = [[] for _ in items]
    high = [[] for _ in items]
    boxes = [box for box, _, _ in forwards]
    reach = max((-(-width // block.shape[dim]) for block, width in items))
    for hop in range(1, reach + 1):
        for sign in (1, -1):
            pieces = []
            owners = []
            for index, (block, width) in enumerate(items):
                size = block.shape[dim]
                rows = min(size, width - (hop - 1) * size)
                if rows <= 0:
                    continue
                begin = size - rows if sign == 1 else 0
                pieces.append(lax.slice_in_dim(block, begin, begin + rows, axis=dim))
                owners.append(index)
            if hop == 1:
                for index, (box, rows_low, rows_high) in enumerate(forwards):
                    rows = rows_low if sign == 1 else rows_high
                    pieces.append(lax.slice_in_dim(box, rows[0], rows[1], axis=dim))
                    owners.append(-1 - index)
            common = [max((p.shape[d] for p in pieces)) for d in (1, 2)]
            joined = jnp.concatenate(
                [
                    jnp.pad(p, ((0, 0), (0, common[0] - p.shape[1]), (0, common[1] - p.shape[2])))
                    for p in pieces
                ],
                axis=0,
            )
            if sign == 1:
                pairs = [(i, i + hop) for i in range(count - hop)]
            else:
                pairs = [(i + hop, i) for i in range(count - hop)]
            got = lax.ppermute(joined, axis, pairs)
            offset = 0
            for index, piece in zip(owners, pieces):
                part = got[offset : offset + piece.shape[0], : piece.shape[1], : piece.shape[2]]
                offset += piece.shape[0]
                if index < 0:
                    box = boxes[-1 - index]
                    parts = [part, box] if sign == 1 else [box, part]
                    boxes[-1 - index] = jnp.concatenate(parts, axis=dim)
                elif sign == 1:
                    low[index].insert(0, part)
                else:
                    high[index].append(part)
    extended = [
        jnp.concatenate(low[i] + [block] + high[i], axis=dim)
        for i, (block, width) in enumerate(items)
    ]
    return (extended, boxes)


def pad_z(box):
    return jnp.pad(box, ((0, 0), (0, 0), (1, 1)))


def trim(box):
    return box[1:-1, 1:-1, :]


def neighbours(padded):
    return [
        padded[2:, 1:-1, 1:-1],
        padded[:-2, 1:-1, 1:-1],
        padded[1:-1, 2:, 1:-1],
        padded[1:-1, :-2, 1:-1],
        padded[1:-1, 1:-1, 2:],
        padded[1:-1, 1:-1, :-2],
    ]


def face_weights(padded_coef, scale):
    centre = padded_coef[1:-1, 1:-1, 1:-1]
    weights = [0.5 * scale * (centre + other) for other in neighbours(padded_coef)]
    diagonal = damping_alpha + weights[0]
    for other in weights[1:]:
        diagonal = diagonal + other
    return (weights, diagonal)


def apply_operator(padded, field, weights, diagonal):
    result = diagonal * field
    for weight, other in zip(weights, neighbours(padded)):
        result = result - weight * other
    return result


def smooth_level(start, right_side, coefficient, scale, extend):
    weights, diagonal = face_weights(extend(coefficient), scale)
    if start is None:
        start = jnp.zeros_like(right_side)
        residual = right_side
    else:
        residual = right_side - apply_operator(extend(start), start, weights, diagonal)
    first_step = residual / (cheb_theta * diagonal)
    first = start + first_step
    residual = right_side - apply_operator(extend(first), first, weights, diagonal)
    second_step = cheb_carry * first_step + cheb_resid * residual / diagonal
    second = first + second_step
    residual = right_side - apply_operator(extend(second), second, weights, diagonal)
    return (second, residual)


def pair_matrix(count):
    rows = jnp.arange(count // 2)[:, None]
    cols = jnp.arange(count)[None, :] // 2
    return (rows == cols).astype(jnp.float32)


def restrict_field(field):
    sx, sy, sz = field.shape
    halves = field.reshape(sx // 2, 2, sy, sz)
    summed = halves[:, 0] + halves[:, 1]
    summed = jnp.einsum("xyZ,zZ->xyz", summed, pair_matrix(sz), precision=lax.Precision.HIGHEST)
    pairs_y = jnp.broadcast_to(pair_matrix(sy), (sx // 2, sy // 2, sy))
    summed = jnp.einsum("xyY,xYz->xyz", pairs_y, summed, precision=lax.Precision.HIGHEST)
    return summed * 0.125


def coarse_solve(right_side, coefficient, scale, extend):
    weights, diagonal = face_weights(extend(coefficient), scale)
    field = jnp.zeros_like(right_side)
    for repeat in range(COARSE_ITERS):
        field = (
            field
            + jacobi_weight
            * (right_side - apply_operator(extend(field), field, weights, diagonal))
            / diagonal
        )
    leftover = right_side - apply_operator(extend(field), field, weights, diagonal)
    ones_field = jnp.ones_like(right_side)
    image_ones = apply_operator(extend(ones_field), ones_field, weights, diagonal)
    return field + jnp.sum(leftover) / jnp.sum(image_ones)


def extend_all(field):
    return jnp.pad(field, 1)


def box_weights(padded_coef, scale):
    centre = padded_coef[1:-1, 1:-1, 1:-1]
    outside = centre == 0.0
    weights = [
        jnp.where(outside, 0.0, 0.5 * scale * (centre + other)) for other in neighbours(padded_coef)
    ]
    diagonal = damping_alpha + weights[0]
    for other in weights[1:]:
        diagonal = diagonal + other
    return (weights, diagonal)


def smooth_box(start, right_side, coefficient, scale):
    weights, diagonal = box_weights(pad_z(coefficient), scale)
    if start is None:
        start = jnp.zeros_like(right_side)
        residual = right_side
    else:
        residual = right_side - apply_operator(pad_z(start), trim(start), weights, diagonal)
        start = trim(start)
    first_step = residual / (cheb_theta * diagonal)
    first = start + first_step
    weights = [trim(w) for w in weights]
    diagonal = trim(diagonal)
    right_side = trim(right_side)
    residual = right_side - apply_operator(pad_z(first), trim(first), weights, diagonal)
    second_step = cheb_carry * trim(first_step) + cheb_resid * residual / diagonal
    second = trim(first) + second_step
    weights = [trim(w) for w in weights]
    diagonal = trim(diagonal)
    residual = trim(right_side) - apply_operator(pad_z(second), trim(second), weights, diagonal)
    return (trim(second), residual)


def collect_grid(right_side, coefficient):
    sx, sy, sz = right_side.shape
    count_x = lax.axis_size("xb")
    count_y = lax.axis_size("yb")
    flat = jnp.concatenate([right_side.reshape(1, -1), coefficient.reshape(1, -1)], axis=1)
    both = lax.all_gather(flat, ("xb", "yb"), axis=0, tiled=True)
    size = sx * sy * sz
    return tuple(
        (
            piece.reshape(count_x, count_y, sx, sy, sz)
            .transpose(0, 2, 1, 3, 4)
            .reshape(count_x * sx, count_y * sy, sz)
            for piece in (both[:, :size], both[:, size:])
        )
    )


def own_block(whole, shape):
    start_x = lax.axis_index("xb") * shape[0]
    start_y = lax.axis_index("yb") * shape[1]
    return lax.dynamic_slice(whole, (start_x, start_y, jnp.int32(0)), shape)


def per_device(initial_guess, right_side, coefficient):
    mid_coef = restrict_field(coefficient)
    low_coef = restrict_field(mid_coef)
    low_size = low_coef.shape[0]
    low_first = min(3, low_size)
    assert low_first == 3 or 2 * low_size >= 3
    guess_b, rhs_b, coef_b, mid_coef_b, low_coef_b = exchange(
        [(initial_guess, 7), (right_side, 7), (coefficient, 7), (mid_coef, 3), (low_coef, 3)],
        "yb",
        1,
    )[0]
    guess_b, rhs_b, coef_b = exchange([(guess_b, 3), (rhs_b, 2), (coef_b, 3)], "xb", 0)[0]
    fine, fine_res = smooth_box(guess_b, rhs_b[:, 1:-1], coef_b, 1.0)
    fine = fine[:, 4:-4]
    mid_rhs = restrict_field(fine_res)
    mid_rhs_b, mid_coef_b, low_coef_b = exchange(
        [(mid_rhs, 2), (mid_coef_b, 3), (low_coef_b, low_first)], "xb", 0
    )[0]
    middle, mid_res = smooth_box(None, mid_rhs_b, mid_coef_b, 0.25)
    low_rhs = restrict_field(mid_res)
    (low_rhs_b,) = exchange([(low_rhs, 3)], "yb", 1)[0]
    forwards = ()
    if low_first < 3:
        forwards = ((low_coef_b, (2 * low_size - 3, low_size), (2 * low_size, low_size + 3)),)
    (low_rhs_b,), boxes = exchange([(low_rhs_b, 2)], "xb", 0, forwards)
    if low_first < 3:
        (low_coef_b,) = boxes
    lower, low_res = smooth_box(None, low_rhs_b[:, 1:-1], low_coef_b, 0.0625)
    coarse_rhs, coarse_coef = collect_grid(restrict_field(low_res), restrict_field(low_coef))
    coarse_whole = coarse_solve(coarse_rhs, coarse_coef, 0.015625, extend_all)
    sx, sy, sz = right_side.shape
    coarse = own_block(coarse_whole, (sx // 8, sy // 8, sz // 8))
    return (fine, middle, lower, coarse)


def solution(mesh):
    placed = (P("xb", "yb", None), P("xb", "yb", None), P("xb", "yb", None))
    return jax.shard_map(
        per_device,
        mesh=mesh,
        in_specs=placed,
        out_specs=(
            P("xb", "yb", None),
            P("xb", "yb", None),
            P("xb", "yb", None),
            P("xb", "yb", None),
        ),
        check_vma=False,
    )
```

profile of v0, /device:TPU:1, one launch (start us, length us, event | category | flops | bytes accessed | tf_op | source)
XLA Modules:
  0.0 128.3 jit_solution(8711913986575202182)
XLA Ops:
  0.7 1.0 slice_dynamic-update-slice_fusion.2
  1.7 1.3 %fusion.218 = f32[4,64,128]{2,1,0:T(8,128)S(1)} fusion(f32[4,2,64,256]{3,2,1,0:T(8,128)} %bitcast.81, s32[256]{0:T(256)S(1)} %and_select_fusion.4), kind=kOutput, calls=%fused_computation.335 | convolution fusion | flops 100761600 | bytes 656384 | tf_op jit(solution)/shard_map/xyZ,zZ->xyz/dot_general | solution.py:134
  3.6 0.9 slice_dynamic-update-slice_fusion.1
  4.5 4.5 %collective-permute-start = (f32[30,7,256]{2,1,0:T(8,128)S(1)}, f32[30,7,256]{2,1,0:T(8,128)S(1)}, u32[]{:S(2)}, u32[]{:S(2)}) collective-permute-start(f32[30,7,256]{2,1,0:T(8,128)S(1)} %constant_dynamic-update-slice_fusion), channel_id=1, source_target_pairs={{0,1},{1,2},{2,3},{3,4},{4,5},{5,6},{6,7},{8,9},{9,10},{10,11},{11... | collective-permute-start | bytes 645128 | tf_op jit(solution)/shard_map/ppermute | solution.py:53
  9.1 1.9 %collective-permute-start.1 = (f32[30,7,256]{2,1,0:T(8,128)S(1)}, f32[30,7,256]{2,1,0:T(8,128)S(1)}, u32[]{:S(2)}, u32[]{:S(2)}) collective-permute-start(f32[30,7,256]{2,1,0:T(8,128)S(1)} %constant_dynamic-update-slice_fusion.2), channel_id=1, source_target_pairs={{1,0},{2,1},{3,2},{4,3},{5,4},{6,5},{7,6},{9,8},{10,9},{11,10},{12... | collective-permute-start | bytes 645128 | tf_op jit(solution)/shard_map/ppermute | solution.py:53
  11.0 1.2 collective-permute-done
  12.6 4.0 %collective-permute-done.1 = f32[30,7,256]{2,1,0:T(8,128)S(1)} collective-permute-done((f32[30,7,256]{2,1,0:T(8,128)S(1)}, f32[30,7,256]{2,1,0:T(8,128)S(1)}, u32[]{:S(2)}, u32[]{:S(2)}) %collective-permute-start.1) | collective-permute-done | bytes 215072 | tf_op jit(solution)/shard_map/ppermute | solution.py:53
  18.5 3.6 %collective-permute-start.2 = (f32[8,78,256]{2,0,1:T(8,128)S(1)}, f32[8,78,256]{2,0,1:T(8,128)S(1)}, u32[]{:S(2)}, u32[]{:S(2)}) collective-permute-start(f32[8,78,256]{2,0,1:T(8,128)S(1)} %pad_maximum_fusion.3), channel_id=1, source_target_pairs={{0,8},{8,16},{16,24},{24,32},{32,40},{40,48},{48,56},{56,64},{64,7... | collective-permute-start | bytes 1916936 | tf_op jit(solution)/shard_map/ppermute | solution.py:53
  22.3 1.3 %collective-permute-start.3 = (f32[8,78,256]{2,0,1:T(8,128)S(1)}, f32[8,78,256]{2,0,1:T(8,128)S(1)}, u32[]{:S(2)}, u32[]{:S(2)}) collective-permute-start(f32[8,78,256]{2,0,1:T(8,128)S(1)} %pad_maximum_fusion.4), channel_id=1, source_target_pairs={{8,0},{16,8},{24,16},{32,24},{40,32},{48,40},{56,48},{64,56},{72,6... | collective-permute-start | bytes 1916936 | tf_op jit(solution)/shard_map/ppermute | solution.py:53
  23.7 8.9 %collective-permute-done.2 = f32[8,78,256]{2,0,1:T(8,128)S(1)} collective-permute-done((f32[8,78,256]{2,0,1:T(8,128)S(1)}, f32[8,78,256]{2,0,1:T(8,128)S(1)}, u32[]{:S(2)}, u32[]{:S(2)}) %collective-permute-start.2) | collective-permute-done | bytes 639008 | tf_op jit(solution)/shard_map/ppermute | solution.py:53
  32.7 4.3 %collective-permute-done.3 = f32[8,78,256]{2,0,1:T(8,128)S(1)} collective-permute-done((f32[8,78,256]{2,0,1:T(8,128)S(1)}, f32[8,78,256]{2,0,1:T(8,128)S(1)}, u32[]{:S(2)}, u32[]{:S(2)}) %collective-permute-start.3) | collective-permute-done | bytes 639008 | tf_op jit(solution)/shard_map/ppermute | solution.py:53
  37.3 1.6 %add_add_fusion = (f32[12,76,256]{2,0,1:T(8,128)S(1)}, f32[12,76,256]{2,0,1:T(8,128)S(1)}, f32[12,76,256]{2,0,1:T(8,128)S(1)}, f32[12,76,256]{2,0,1:T(8,128)S(1)...) fusion(f32[14,78,256]{2,0,1:T(8,128)S(1)} %pad_maximum_fusion.2), kind=kLoop, calls=%fused_computation.55 | loop fusion | flops 5836800 | bytes 14041088 | tf_op jit(solution)/shard_map/add | solution.py:168
  39.5 2.1 %slice_add_fusion.4 = (f32[12,76,256]{2,0,1:T(8,128)S(1)}, f32[12,76,256]{2,0,1:T(8,128)S(1)}) fusion(f32[14,78,256]{2,0,1:T(8,128)S(1)} %pad_maximum_fusion, f32[12,76,256]{2,0,1:T(8,128)S(1)} %get-tuple-element.42, f32[12,76,256]{2,0,1:T(8,128)S(1)} %get-tuple-element.43, f32[12,76,256]{2,0,1:T(8,128)S(1)} %get-tuple-element.41, ...), kind=kLoop, calls=%fused_computation.74 | loop fusion | flops 5369856 | bytes 18087936 | tf_op jit(solution)/shard_map/add | solution.py:181
  41.6 2.4 %fusion.31 = f32[10,74,256]{2,0,1:T(8,128)S(1)} fusion(f32[12,76,256]{2,0,1:T(8,128)S(1)} %get-tuple-element.44, f32[12,76,256]{2,0,1:T(8,128)S(1)} %get-tuple-element.42, f32[12,76,256]{2,0,1:T(8,128)S(1)} %get-tuple-element.43, f32[12,76,256]{2,0,1:T(8,128)S(1)} %get-tuple-element.41, f32[12,76,256]{2,0,1:T(8,128)S(1)} %get-tuple-element.40, ...), kind=kLoop, calls=%fused_computation.63 | loop fusion | flops 3599360 | bytes 18976768 | tf_op jit(solution)/shard_map/add | solution.py:187
  44.0 0.9 fusion.40
  46.5 3.5 %collective-permute-start.4 = (f32[7,38,128]{2,1,0:T(8,128)S(1)}, f32[7,38,128]{2,1,0:T(8,128)S(1)}, u32[]{:S(2)}, u32[]{:S(2)}) collective-permute-start(f32[7,38,128]{2,1,0:T(8,128)S(1)} %get-tuple-element.89), channel_id=1, source_target_pairs={{0,8},{8,16},{16,24},{24,32},{32,40},{40,48},{48,56},{56,64},{64,7... | collective-permute-start | bytes 408584 | tf_op jit(solution)/shard_map/ppermute | solution.py:53
  50.0 1.3 %collective-permute-start.5 = (f32[7,38,128]{2,1,0:T(8,128)S(1)}, f32[7,38,128]{2,1,0:T(8,128)S(1)}, u32[]{:S(2)}, u32[]{:S(2)}) collective-permute-start(f32[7,38,128]{2,1,0:T(8,128)S(1)} %get-tuple-element.90), channel_id=1, source_target_pairs={{8,0},{16,8},{24,16},{32,24},{40,32},{48,40},{56,48},{64,56},{72,6... | collective-permute-start | bytes 408584 | tf_op jit(solution)/shard_map/ppermute | solution.py:53
  52.0 3.8 %collective-permute-done.5 = f32[7,38,128]{2,1,0:T(8,128)S(1)} collective-permute-done((f32[7,38,128]{2,1,0:T(8,128)S(1)}, f32[7,38,128]{2,1,0:T(8,128)S(1)}, u32[]{:S(2)}, u32[]{:S(2)}) %collective-permute-start.5) | collective-permute-done | bytes 136224 | tf_op jit(solution)/shard_map/ppermute | solution.py:53
  56.3 0.7 fusion.272
  57.3 8.1 %collective-permute-start.6 = (f32[2,3,64]{2,1,0:T(4,128)S(1)}, f32[2,3,64]{2,1,0:T(4,128)S(1)}, u32[]{:S(2)}, u32[]{:S(2)}) collective-permute-start(f32[2,3,64]{2,1,0:T(4,128)S(1)} %get-tuple-element.91), channel_id=1, source_target_pairs={{0,1},{1,2},{2,3},{3,4},{4,5},{5,6},{6,7},{8,9},{9,10},{10,11},{11... | collective-permute-start | bytes 4616 | tf_op jit(solution)/shard_map/ppermute | solution.py:53
  65.4 1.9 %collective-permute-start.7 = (f32[2,3,64]{2,1,0:T(4,128)S(1)}, f32[2,3,64]{2,1,0:T(4,128)S(1)}, u32[]{:S(2)}, u32[]{:S(2)}) collective-permute-start(f32[2,3,64]{2,1,0:T(4,128)S(1)} %get-tuple-element.92), channel_id=1, source_target_pairs={{1,0},{2,1},{3,2},{4,3},{5,4},{6,5},{7,6},{9,8},{10,9},{11,10},{12... | collective-permute-start | bytes 4616 | tf_op jit(solution)/shard_map/ppermute | solution.py:53
  67.4 3.0 %collective-permute-done.7 = f32[2,3,64]{2,1,0:T(4,128)S(1)} collective-permute-done((f32[2,3,64]{2,1,0:T(4,128)S(1)}, f32[2,3,64]{2,1,0:T(4,128)S(1)}, u32[]{:S(2)}, u32[]{:S(2)}) %collective-permute-start.7) | collective-permute-done | bytes 1568 | tf_op jit(solution)/shard_map/ppermute | solution.py:53
  70.4 3.8 %collective-permute-start.8 = (f32[3,22,64]{2,1,0:T(8,128)S(1)}, f32[3,22,64]{2,1,0:T(8,128)S(1)}, u32[]{:S(2)}, u32[]{:S(2)}) collective-permute-start(f32[3,22,64]{2,1,0:T(8,128)S(1)} %get-tuple-element.87), channel_id=1, source_target_pairs={{0,8},{8,16},{16,24},{24,32},{32,40},{40,48},{48,56},{56,64},{64,7... | collective-permute-start | bytes 50696 | tf_op jit(solution)/shard_map/ppermute | solution.py:53
  74.5 1.0 copy.24
  75.4 1.5 %collective-permute-start.9 = (f32[3,22,64]{2,1,0:T(8,128)S(1)}, f32[3,22,64]{2,1,0:T(8,128)S(1)}, u32[]{:S(2)}, u32[]{:S(2)}) collective-permute-start(f32[3,22,64]{2,1,0:T(8,128)S(1)} %get-tuple-element.88), channel_id=1, source_target_pairs={{8,0},{16,8},{24,16},{32,24},{40,32},{48,40},{56,48},{64,56},{72,6... | collective-permute-start | bytes 50696 | tf_op jit(solution)/shard_map/ppermute | solution.py:53
  77.0 3.1 %collective-permute-done.9 = f32[3,22,64]{2,1,0:T(8,128)S(1)} collective-permute-done((f32[3,22,64]{2,1,0:T(8,128)S(1)}, f32[3,22,64]{2,1,0:T(8,128)S(1)}, u32[]{:S(2)}, u32[]{:S(2)}) %collective-permute-start.9) | collective-permute-done | bytes 16928 | tf_op jit(solution)/shard_map/ppermute | solution.py:53
  81.4 37.1 %all-gather = f32[128,1,512]{2,1,0:T(1,128)S(1)} all-gather(f32[1,1,512]{2,1,0:T(1,128)S(1)} %maximum_bitcast_fusion), channel_id=1, replica_groups=mesh['xb'=16,'yb'=8] {'xb','yb'}, dimensions={0}, use_global_device_ids=true | all-gather | bytes 264192 | tf_op jit(solution)/shard_map/all_gather | solution.py:199
  118.9 1.0 fusion.192
  120.6 0.7 fusion.84
  121.3 0.7 fusion.100
  122.0 0.7 fusion.116
  124.8 1.6 %fusion.210 = (f32[]{:T(128)}, f32[]{:T(128)}) fusion(f32[16,64,32]{2,1,0:T(8,128)S(1)} %get-tuple-element.11, f32[16,64,32]{2,1,0:T(8,128)S(1)} %broadcast_in_dim.37, f32[16,64,32]{2,1,0:T(8,128)S(1)} %get-tuple-element.12, f32[16,64,32]{2,1,0:T(8,128)S(1)} %get-tuple-element.13, f32[16,64,32]{2,1,0:T(8,128)S(1)} %get-tuple-element.14, ...), kind=kLoop, calls=%fused_computation.320 | loop fusion | flops 1114110 | bytes 1179656 | tf_op jit(solution)/shard_map/reduce_sum | solution.py:153
  (107 shorter events, 12.5 us)
Async XLA Ops:
  0.6 3.9 %copy-start = (f32[8,64,256]{2,1,0:T(8,128)S(1)}, f32[8,64,256]{2,1,0:T(8,128)}, u32[]{:S(2)}) copy-start(f32[8,64,256]{2,1,0:T(8,128)} %param.5) | copy-start | bytes 1572868
  0.6 11.6 %copy-start.1 = (f32[8,64,256]{2,1,0:T(8,128)S(1)}, f32[8,64,256]{2,1,0:T(8,128)}, u32[]{:S(2)}) copy-start(f32[8,64,256]{2,1,0:T(8,128)} %param.4) | copy-start | bytes 1572868
  4.5 7.6 %collective-permute-start = (f32[30,7,256]{2,1,0:T(8,128)S(1)}, f32[30,7,256]{2,1,0:T(8,128)S(1)}, u32[]{:S(2)}, u32[]{:S(2)}) collective-permute-start(f32[30,7,256]{2,1,0:T(8,128)S(1)} %constant_dynamic-update-slice_fusion), channel_id=1, source_target_pairs={{0,1},{1,2},{2,3},{3,4},{4,5},{5,6},{6,7},{8,9},{9,10},{10,11},{11... | collective-permute-start | bytes 645128 | tf_op jit(solution)/shard_map/ppermute | solution.py:53
  9.1 7.5 %collective-permute-start.1 = (f32[30,7,256]{2,1,0:T(8,128)S(1)}, f32[30,7,256]{2,1,0:T(8,128)S(1)}, u32[]{:S(2)}, u32[]{:S(2)}) collective-permute-start(f32[30,7,256]{2,1,0:T(8,128)S(1)} %constant_dynamic-update-slice_fusion.2), channel_id=1, source_target_pairs={{1,0},{2,1},{3,2},{4,3},{5,4},{6,5},{7,6},{9,8},{10,9},{11,10},{12... | collective-permute-start | bytes 645128 | tf_op jit(solution)/shard_map/ppermute | solution.py:53
  16.7 1.0 copy-start.2
  18.5 14.1 %collective-permute-start.2 = (f32[8,78,256]{2,0,1:T(8,128)S(1)}, f32[8,78,256]{2,0,1:T(8,128)S(1)}, u32[]{:S(2)}, u32[]{:S(2)}) collective-permute-start(f32[8,78,256]{2,0,1:T(8,128)S(1)} %pad_maximum_fusion.3), channel_id=1, source_target_pairs={{0,8},{8,16},{16,24},{24,32},{32,40},{40,48},{48,56},{56,64},{64,7... | collective-permute-start | bytes 1916936 | tf_op jit(solution)/shard_map/ppermute | solution.py:53
  22.3 14.6 %collective-permute-start.3 = (f32[8,78,256]{2,0,1:T(8,128)S(1)}, f32[8,78,256]{2,0,1:T(8,128)S(1)}, u32[]{:S(2)}, u32[]{:S(2)}) collective-permute-start(f32[8,78,256]{2,0,1:T(8,128)S(1)} %pad_maximum_fusion.4), channel_id=1, source_target_pairs={{8,0},{16,8},{24,16},{32,24},{40,32},{48,40},{56,48},{64,56},{72,6... | collective-permute-start | bytes 1916936 | tf_op jit(solution)/shard_map/ppermute | solution.py:53
  46.5 5.6 %collective-permute-start.4 = (f32[7,38,128]{2,1,0:T(8,128)S(1)}, f32[7,38,128]{2,1,0:T(8,128)S(1)}, u32[]{:S(2)}, u32[]{:S(2)}) collective-permute-start(f32[7,38,128]{2,1,0:T(8,128)S(1)} %get-tuple-element.89), channel_id=1, source_target_pairs={{0,8},{8,16},{16,24},{24,32},{32,40},{40,48},{48,56},{56,64},{64,7... | collective-permute-start | bytes 408584 | tf_op jit(solution)/shard_map/ppermute | solution.py:53
  50.0 5.8 %collective-permute-start.5 = (f32[7,38,128]{2,1,0:T(8,128)S(1)}, f32[7,38,128]{2,1,0:T(8,128)S(1)}, u32[]{:S(2)}, u32[]{:S(2)}) collective-permute-start(f32[7,38,128]{2,1,0:T(8,128)S(1)} %get-tuple-element.90), channel_id=1, source_target_pairs={{8,0},{16,8},{24,16},{32,24},{40,32},{48,40},{56,48},{64,56},{72,6... | collective-permute-start | bytes 408584 | tf_op jit(solution)/shard_map/ppermute | solution.py:53
  57.3 10.0 %collective-permute-start.6 = (f32[2,3,64]{2,1,0:T(4,128)S(1)}, f32[2,3,64]{2,1,0:T(4,128)S(1)}, u32[]{:S(2)}, u32[]{:S(2)}) collective-permute-start(f32[2,3,64]{2,1,0:T(4,128)S(1)} %get-tuple-element.91), channel_id=1, source_target_pairs={{0,1},{1,2},{2,3},{3,4},{4,5},{5,6},{6,7},{8,9},{9,10},{10,11},{11... | collective-permute-start | bytes 4616 | tf_op jit(solution)/shard_map/ppermute | solution.py:53
  65.4 4.9 %collective-permute-start.7 = (f32[2,3,64]{2,1,0:T(4,128)S(1)}, f32[2,3,64]{2,1,0:T(4,128)S(1)}, u32[]{:S(2)}, u32[]{:S(2)}) collective-permute-start(f32[2,3,64]{2,1,0:T(4,128)S(1)} %get-tuple-element.92), channel_id=1, source_target_pairs={{1,0},{2,1},{3,2},{4,3},{5,4},{6,5},{7,6},{9,8},{10,9},{11,10},{12... | collective-permute-start | bytes 4616 | tf_op jit(solution)/shard_map/ppermute | solution.py:53
  70.4 6.6 %collective-permute-start.8 = (f32[3,22,64]{2,1,0:T(8,128)S(1)}, f32[3,22,64]{2,1,0:T(8,128)S(1)}, u32[]{:S(2)}, u32[]{:S(2)}) collective-permute-start(f32[3,22,64]{2,1,0:T(8,128)S(1)} %get-tuple-element.87), channel_id=1, source_target_pairs={{0,8},{8,16},{16,24},{24,32},{32,40},{40,48},{48,56},{56,64},{64,7... | collective-permute-start | bytes 50696 | tf_op jit(solution)/shard_map/ppermute | solution.py:53
  75.4 4.7 %collective-permute-start.9 = (f32[3,22,64]{2,1,0:T(8,128)S(1)}, f32[3,22,64]{2,1,0:T(8,128)S(1)}, u32[]{:S(2)}, u32[]{:S(2)}) collective-permute-start(f32[3,22,64]{2,1,0:T(8,128)S(1)} %get-tuple-element.88), channel_id=1, source_target_pairs={{8,0},{16,8},{24,16},{32,24},{40,32},{48,40},{56,48},{64,56},{72,6... | collective-permute-start | bytes 50696 | tf_op jit(solution)/shard_map/ppermute | solution.py:53
where the time goes:
time: 129 us; the launch traced here: 128 us
  blocking collectives  37.1 us (29%)
  starting transfers between devices  31.4 us (24%)
  waiting for transfers between devices  28.8 us (22%)
  other arithmetic  18.3 us (14%)
  local copies, waits for them, and re-layouts  6.72 us (5%)
  matrix products  3.27 us (3%)
  between operations  2.68 us (2%)
    all_gather x1, blocking collectives, collect_grid(): both = lax.all_gather(flat, ('xb', 'yb'), axis=0, tiled=True)  37.1 us
    ppermute x10, starting transfers between devices, exchange(): got = lax.ppermute(joined, axis, pairs)  31.4 us
    ppermute x10, waiting for transfers between devices, exchange(): got = lax.ppermute(joined, axis, pairs)  28.8 us
    add x7, other arithmetic, coarse_solve(): field + jacobi_weight * (right_side - apply_operator(extend(field), field...  4.78 us
    unnamed x21, local copies, waits for them, and re-layouts  4.42 us
    add x3, other arithmetic, smooth_box(): second = trim(first) + second_step  2.77 us
  transfers between devices with their start and end apart: 10, of which 8 were waited for; matrix products, arithmetic and copies ran while one was open for 2% of the time, Pallas kernels for 0%

commit v1 on v0

--- a/solution.py
+++ b/solution.py
@@ -196,7 +196,9 @@
     count_x = lax.axis_size("xb")
     count_y = lax.axis_size("yb")
     flat = jnp.concatenate([right_side.reshape(1, -1), coefficient.reshape(1, -1)], axis=1)
-    both = lax.all_gather(flat, ("xb", "yb"), axis=0, tiled=True)
+    both = jnp.concatenate(
+        lax.all_to_all(jnp.stack([flat] * lax.axis_size(("xb", "yb"))), ("xb", "yb"), 0, 0), axis=0
+    )
     size = sx * sy * sz
     return tuple(
         (

time: 129 us -> 114 us (0.88)
  blocking collectives: 37.1 us -> 0 us
  starting transfers between devices: 31.4 us -> 42.4 us
  waiting for transfers between devices: 28.8 us -> 38.8 us
    all_gather x1 -> x0, blocking collectives: 37.1 us -> none  [collect_grid(): both = lax.all_gather(flat, ('xb', 'yb'), axis=0, tiled=True)]
    all_to_all x0 -> x1, starting transfers between devices: none -> 11 us  [collect_grid(): lax.all_to_all(jnp.stack([flat] * lax.axis_size(('xb', 'yb'))), ('xb', 'y...]
    all_to_all x0 -> x1, waiting for transfers between devices: none -> 9.98 us  [collect_grid(): lax.all_to_all(jnp.stack([flat] * lax.axis_size(('xb', 'yb'))), ('xb', 'y...]
  transfers between devices with their start and end apart: 10 -> 11, of which waited for: 8 -> 9; matrix products, arithmetic and copies ran while one was open for 2% -> 2% of each run, Pallas kernels for 0% -> 0%
where the time goes in v1:
time: 114 us; the launch traced here: 113 us
  starting transfers between devices  42.4 us (37%)
  waiting for transfers between devices  38.8 us (34%)
  other arithmetic  18.3 us (16%)
  local copies, waits for them, and re-layouts  7.58 us (7%)
  matrix products  3.28 us (3%)
  between operations  2.71 us (2%)
    ppermute x10, starting transfers between devices, exchange(): got = lax.ppermute(joined, axis, pairs)  31.4 us
    ppermute x10, waiting for transfers between devices, exchange(): got = lax.ppermute(joined, axis, pairs)  28.8 us
    all_to_all x1, starting transfers between devices, collect_grid(): lax.all_to_all(jnp.stack([flat] * lax.axis_size(('xb', 'yb'))), ('xb', 'y...  11 us
    all_to_all x1, waiting for transfers between devices, collect_grid(): lax.all_to_all(jnp.stack([flat] * lax.axis_size(('xb', 'yb'))), ('xb', 'y...  9.98 us
    add x7, other arithmetic, coarse_solve(): field + jacobi_weight * (right_side - apply_operator(extend(field), field...  4.78 us
    unnamed x21, local copies, waits for them, and re-layouts  4.42 us
    add x3, other arithmetic, smooth_box(): second = trim(first) + second_step  2.77 us
  transfers between devices with their start and end apart: 11, of which 9 were waited for; matrix products, arithmetic and copies ran while one was open for 2% of the time, Pallas kernels for 0%

profile of v1, /device:TPU:1, one launch (start us, length us, event | category | flops | bytes accessed | tf_op | source)
XLA Modules:
  0.0 113.0 jit_solution(6935233193139851123)
XLA Ops:
  0.7 1.0 slice_dynamic-update-slice_fusion.2
  1.7 1.3 %fusion.218 = f32[4,64,128]{2,1,0:T(8,128)S(1)} fusion(f32[4,2,64,256]{3,2,1,0:T(8,128)} %bitcast.80, s32[256]{0:T(256)S(1)} %and_select_fusion.4), kind=kOutput, calls=%fused_computation.335 | convolution fusion | flops 100761600 | bytes 656384 | tf_op jit(solution)/shard_map/xyZ,zZ->xyz/dot_general | solution.py:134
  3.6 0.9 slice_dynamic-update-slice_fusion.1
  4.5 4.5 %collective-permute-start = (f32[30,7,256]{2,1,0:T(8,128)S(1)}, f32[30,7,256]{2,1,0:T(8,128)S(1)}, u32[]{:S(2)}, u32[]{:S(2)}) collective-permute-start(f32[30,7,256]{2,1,0:T(8,128)S(1)} %constant_dynamic-update-slice_fusion), channel_id=1, source_target_pairs={{0,1},{1,2},{2,3},{3,4},{4,5},{5,6},{6,7},{8,9},{9,10},{10,11},{11... | collective-permute-start | bytes 645128 | tf_op jit(solution)/shard_map/ppermute | solution.py:53
  9.1 1.9 %collective-permute-start.1 = (f32[30,7,256]{2,1,0:T(8,128)S(1)}, f32[30,7,256]{2,1,0:T(8,128)S(1)}, u32[]{:S(2)}, u32[]{:S(2)}) collective-permute-start(f32[30,7,256]{2,1,0:T(8,128)S(1)} %constant_dynamic-update-slice_fusion.2), channel_id=1, source_target_pairs={{1,0},{2,1},{3,2},{4,3},{5,4},{6,5},{7,6},{9,8},{10,9},{11,10},{12... | collective-permute-start | bytes 645128 | tf_op jit(solution)/shard_map/ppermute | solution.py:53
  11.0 1.2 %collective-permute-done = f32[30,7,256]{2,1,0:T(8,128)S(1)} collective-permute-done((f32[30,7,256]{2,1,0:T(8,128)S(1)}, f32[30,7,256]{2,1,0:T(8,128)S(1)}, u32[]{:S(2)}, u32[]{:S(2)}) %collective-permute-start) | collective-permute-done | bytes 215072 | tf_op jit(solution)/shard_map/ppermute | solution.py:53
  12.6 4.0 %collective-permute-done.1 = f32[30,7,256]{2,1,0:T(8,128)S(1)} collective-permute-done((f32[30,7,256]{2,1,0:T(8,128)S(1)}, f32[30,7,256]{2,1,0:T(8,128)S(1)}, u32[]{:S(2)}, u32[]{:S(2)}) %collective-permute-start.1) | collective-permute-done | bytes 215072 | tf_op jit(solution)/shard_map/ppermute | solution.py:53
  18.5 3.6 %collective-permute-start.2 = (f32[8,78,256]{2,0,1:T(8,128)S(1)}, f32[8,78,256]{2,0,1:T(8,128)S(1)}, u32[]{:S(2)}, u32[]{:S(2)}) collective-permute-start(f32[8,78,256]{2,0,1:T(8,128)S(1)} %pad_maximum_fusion.3), channel_id=1, source_target_pairs={{0,8},{8,16},{16,24},{24,32},{32,40},{40,48},{48,56},{56,64},{64,7... | collective-permute-start | bytes 1916936 | tf_op jit(solution)/shard_map/ppermute | solution.py:53
  22.3 1.3 %collective-permute-start.3 = (f32[8,78,256]{2,0,1:T(8,128)S(1)}, f32[8,78,256]{2,0,1:T(8,128)S(1)}, u32[]{:S(2)}, u32[]{:S(2)}) collective-permute-start(f32[8,78,256]{2,0,1:T(8,128)S(1)} %pad_maximum_fusion.4), channel_id=1, source_target_pairs={{8,0},{16,8},{24,16},{32,24},{40,32},{48,40},{56,48},{64,56},{72,6... | collective-permute-start | bytes 1916936 | tf_op jit(solution)/shard_map/ppermute | solution.py:53
  23.7 8.9 %collective-permute-done.2 = f32[8,78,256]{2,0,1:T(8,128)S(1)} collective-permute-done((f32[8,78,256]{2,0,1:T(8,128)S(1)}, f32[8,78,256]{2,0,1:T(8,128)S(1)}, u32[]{:S(2)}, u32[]{:S(2)}) %collective-permute-start.2) | collective-permute-done | bytes 639008 | tf_op jit(solution)/shard_map/ppermute | solution.py:53
  32.7 4.3 %collective-permute-done.3 = f32[8,78,256]{2,0,1:T(8,128)S(1)} collective-permute-done((f32[8,78,256]{2,0,1:T(8,128)S(1)}, f32[8,78,256]{2,0,1:T(8,128)S(1)}, u32[]{:S(2)}, u32[]{:S(2)}) %collective-permute-start.3) | collective-permute-done | bytes 639008 | tf_op jit(solution)/shard_map/ppermute | solution.py:53
  37.3 1.6 %add_add_fusion = (f32[12,76,256]{2,0,1:T(8,128)S(1)}, f32[12,76,256]{2,0,1:T(8,128)S(1)}, f32[12,76,256]{2,0,1:T(8,128)S(1)}, f32[12,76,256]{2,0,1:T(8,128)S(1)...) fusion(f32[14,78,256]{2,0,1:T(8,128)S(1)} %pad_maximum_fusion.2), kind=kLoop, calls=%fused_computation.55 | loop fusion | flops 5836800 | bytes 14041088 | tf_op jit(solution)/shard_map/add | solution.py:168
  39.5 2.1 %slice_add_fusion.4 = (f32[12,76,256]{2,0,1:T(8,128)S(1)}, f32[12,76,256]{2,0,1:T(8,128)S(1)}) fusion(f32[14,78,256]{2,0,1:T(8,128)S(1)} %pad_maximum_fusion, f32[12,76,256]{2,0,1:T(8,128)S(1)} %get-tuple-element.42, f32[12,76,256]{2,0,1:T(8,128)S(1)} %get-tuple-element.43, f32[12,76,256]{2,0,1:T(8,128)S(1)} %get-tuple-element.41, ...), kind=kLoop, calls=%fused_computation.74 | loop fusion | flops 5369856 | bytes 18087936 | tf_op jit(solution)/shard_map/add | solution.py:181
  41.6 2.4 %fusion.31 = f32[10,74,256]{2,0,1:T(8,128)S(1)} fusion(f32[12,76,256]{2,0,1:T(8,128)S(1)} %get-tuple-element.44, f32[12,76,256]{2,0,1:T(8,128)S(1)} %get-tuple-element.42, f32[12,76,256]{2,0,1:T(8,128)S(1)} %get-tuple-element.43, f32[12,76,256]{2,0,1:T(8,128)S(1)} %get-tuple-element.41, f32[12,76,256]{2,0,1:T(8,128)S(1)} %get-tuple-element.40, ...), kind=kLoop, calls=%fused_computation.63 | loop fusion | flops 3599360 | bytes 18976768 | tf_op jit(solution)/shard_map/add | solution.py:187
  44.0 0.9 fusion.40
  46.5 3.5 %collective-permute-start.4 = (f32[7,38,128]{2,1,0:T(8,128)S(1)}, f32[7,38,128]{2,1,0:T(8,128)S(1)}, u32[]{:S(2)}, u32[]{:S(2)}) collective-permute-start(f32[7,38,128]{2,1,0:T(8,128)S(1)} %get-tuple-element.89), channel_id=1, source_target_pairs={{0,8},{8,16},{16,24},{24,32},{32,40},{40,48},{48,56},{56,64},{64,7... | collective-permute-start | bytes 408584 | tf_op jit(solution)/shard_map/ppermute | solution.py:53
  50.0 1.3 %collective-permute-start.5 = (f32[7,38,128]{2,1,0:T(8,128)S(1)}, f32[7,38,128]{2,1,0:T(8,128)S(1)}, u32[]{:S(2)}, u32[]{:S(2)}) collective-permute-start(f32[7,38,128]{2,1,0:T(8,128)S(1)} %get-tuple-element.90), channel_id=1, source_target_pairs={{8,0},{16,8},{24,16},{32,24},{40,32},{48,40},{56,48},{64,56},{72,6... | collective-permute-start | bytes 408584 | tf_op jit(solution)/shard_map/ppermute | solution.py:53
  52.0 3.8 %collective-permute-done.5 = f32[7,38,128]{2,1,0:T(8,128)S(1)} collective-permute-done((f32[7,38,128]{2,1,0:T(8,128)S(1)}, f32[7,38,128]{2,1,0:T(8,128)S(1)}, u32[]{:S(2)}, u32[]{:S(2)}) %collective-permute-start.5) | collective-permute-done | bytes 136224 | tf_op jit(solution)/shard_map/ppermute | solution.py:53
  56.3 0.7 fusion.272
  57.3 8.1 %collective-permute-start.6 = (f32[2,3,64]{2,1,0:T(4,128)S(1)}, f32[2,3,64]{2,1,0:T(4,128)S(1)}, u32[]{:S(2)}, u32[]{:S(2)}) collective-permute-start(f32[2,3,64]{2,1,0:T(4,128)S(1)} %get-tuple-element.91), channel_id=1, source_target_pairs={{0,1},{1,2},{2,3},{3,4},{4,5},{5,6},{6,7},{8,9},{9,10},{10,11},{11... | collective-permute-start | bytes 4616 | tf_op jit(solution)/shard_map/ppermute | solution.py:53
  65.4 1.9 %collective-permute-start.7 = (f32[2,3,64]{2,1,0:T(4,128)S(1)}, f32[2,3,64]{2,1,0:T(4,128)S(1)}, u32[]{:S(2)}, u32[]{:S(2)}) collective-permute-start(f32[2,3,64]{2,1,0:T(4,128)S(1)} %get-tuple-element.92), channel_id=1, source_target_pairs={{1,0},{2,1},{3,2},{4,3},{5,4},{6,5},{7,6},{9,8},{10,9},{11,10},{12... | collective-permute-start | bytes 4616 | tf_op jit(solution)/shard_map/ppermute | solution.py:53
  67.4 3.0 %collective-permute-done.7 = f32[2,3,64]{2,1,0:T(4,128)S(1)} collective-permute-done((f32[2,3,64]{2,1,0:T(4,128)S(1)}, f32[2,3,64]{2,1,0:T(4,128)S(1)}, u32[]{:S(2)}, u32[]{:S(2)}) %collective-permute-start.7) | collective-permute-done | bytes 1568 | tf_op jit(solution)/shard_map/ppermute | solution.py:53
  70.4 3.8 %collective-permute-start.8 = (f32[3,22,64]{2,1,0:T(8,128)S(1)}, f32[3,22,64]{2,1,0:T(8,128)S(1)}, u32[]{:S(2)}, u32[]{:S(2)}) collective-permute-start(f32[3,22,64]{2,1,0:T(8,128)S(1)} %get-tuple-element.87), channel_id=1, source_target_pairs={{0,8},{8,16},{16,24},{24,32},{32,40},{40,48},{48,56},{56,64},{64,7... | collective-permute-start | bytes 50696 | tf_op jit(solution)/shard_map/ppermute | solution.py:53
  74.4 1.5 %collective-permute-start.9 = (f32[3,22,64]{2,1,0:T(8,128)S(1)}, f32[3,22,64]{2,1,0:T(8,128)S(1)}, u32[]{:S(2)}, u32[]{:S(2)}) collective-permute-start(f32[3,22,64]{2,1,0:T(8,128)S(1)} %get-tuple-element.88), channel_id=1, source_target_pairs={{8,0},{16,8},{24,16},{32,24},{40,32},{48,40},{56,48},{64,56},{72,6... | collective-permute-start | bytes 50696 | tf_op jit(solution)/shard_map/ppermute | solution.py:53
  76.0 3.1 %collective-permute-done.9 = f32[3,22,64]{2,1,0:T(8,128)S(1)} collective-permute-done((f32[3,22,64]{2,1,0:T(8,128)S(1)}, f32[3,22,64]{2,1,0:T(8,128)S(1)}, u32[]{:S(2)}, u32[]{:S(2)}) %collective-permute-start.9) | collective-permute-done | bytes 16928 | tf_op jit(solution)/shard_map/ppermute | solution.py:53
  80.4 0.9 stack.2
  81.2 11.0 %all-to-all-start = ((f32[128,1,512]{2,1,0:T(1,128)}), f32[128,1,512]{2,1,0:T(1,128)S(1)}, u32[]{:S(2)}, u32[]{:S(2)}) async-start(f32[128,1,512]{2,1,0:T(1,128)} %stack.2), calls=%async_computation | async-start | bytes 524288 | tf_op jit(solution)/shard_map/all_to_all | solution.py:200
  92.3 1.0 copy.24
  93.2 10.0 %all-to-all-done = f32[128,1,512]{2,1,0:T(1,128)S(1)} async-done(((f32[128,1,512]{2,1,0:T(1,128)}), f32[128,1,512]{2,1,0:T(1,128)S(1)}, u32[]{:S(2)}, u32[]{:S(2)}) %all-to-all-start) | async-done | bytes 262176 | tf_op jit(solution)/shard_map/all_to_all | solution.py:200
  103.7 1.0 fusion.192
  106.0 0.7 fusion.100
  109.5 1.6 %fusion.210 = (f32[]{:T(128)}, f32[]{:T(128)}) fusion(f32[16,64,32]{2,1,0:T(8,128)S(1)} %get-tuple-element.11, f32[16,64,32]{2,1,0:T(8,128)S(1)} %broadcast_in_dim.37, f32[16,64,32]{2,1,0:T(8,128)S(1)} %get-tuple-element.12, f32[16,64,32]{2,1,0:T(8,128)S(1)} %get-tuple-element.13, f32[16,64,32]{2,1,0:T(8,128)S(1)} %get-tuple-element.14, ...), kind=kLoop, calls=%fused_computation.320 | loop fusion | flops 1114110 | bytes 1179656 | tf_op jit(solution)/shard_map/reduce_sum | solution.py:153
  (109 shorter events, 13.8 us)
Async XLA Ops:
  0.6 3.9 %copy-start = (f32[8,64,256]{2,1,0:T(8,128)S(1)}, f32[8,64,256]{2,1,0:T(8,128)}, u32[]{:S(2)}) copy-start(f32[8,64,256]{2,1,0:T(8,128)} %param.5) | copy-start | bytes 1572868
  0.6 11.6 %copy-start.1 = (f32[8,64,256]{2,1,0:T(8,128)S(1)}, f32[8,64,256]{2,1,0:T(8,128)}, u32[]{:S(2)}) copy-start(f32[8,64,256]{2,1,0:T(8,128)} %param.4) | copy-start | bytes 1572868
  4.5 7.6 %collective-permute-start = (f32[30,7,256]{2,1,0:T(8,128)S(1)}, f32[30,7,256]{2,1,0:T(8,128)S(1)}, u32[]{:S(2)}, u32[]{:S(2)}) collective-permute-start(f32[30,7,256]{2,1,0:T(8,128)S(1)} %constant_dynamic-update-slice_fusion), channel_id=1, source_target_pairs={{0,1},{1,2},{2,3},{3,4},{4,5},{5,6},{6,7},{8,9},{9,10},{10,11},{11... | collective-permute-start | bytes 645128 | tf_op jit(solution)/shard_map/ppermute | solution.py:53
  9.1 7.5 %collective-permute-start.1 = (f32[30,7,256]{2,1,0:T(8,128)S(1)}, f32[30,7,256]{2,1,0:T(8,128)S(1)}, u32[]{:S(2)}, u32[]{:S(2)}) collective-permute-start(f32[30,7,256]{2,1,0:T(8,128)S(1)} %constant_dynamic-update-slice_fusion.2), channel_id=1, source_target_pairs={{1,0},{2,1},{3,2},{4,3},{5,4},{6,5},{7,6},{9,8},{10,9},{11,10},{12... | collective-permute-start | bytes 645128 | tf_op jit(solution)/shard_map/ppermute | solution.py:53
  16.7 1.0 copy-start.2
  18.5 14.1 %collective-permute-start.2 = (f32[8,78,256]{2,0,1:T(8,128)S(1)}, f32[8,78,256]{2,0,1:T(8,128)S(1)}, u32[]{:S(2)}, u32[]{:S(2)}) collective-permute-start(f32[8,78,256]{2,0,1:T(8,128)S(1)} %pad_maximum_fusion.3), channel_id=1, source_target_pairs={{0,8},{8,16},{16,24},{24,32},{32,40},{40,48},{48,56},{56,64},{64,7... | collective-permute-start | bytes 1916936 | tf_op jit(solution)/shard_map/ppermute | solution.py:53
  22.3 14.6 %collective-permute-start.3 = (f32[8,78,256]{2,0,1:T(8,128)S(1)}, f32[8,78,256]{2,0,1:T(8,128)S(1)}, u32[]{:S(2)}, u32[]{:S(2)}) collective-permute-start(f32[8,78,256]{2,0,1:T(8,128)S(1)} %pad_maximum_fusion.4), channel_id=1, source_target_pairs={{8,0},{16,8},{24,16},{32,24},{40,32},{48,40},{56,48},{64,56},{72,6... | collective-permute-start | bytes 1916936 | tf_op jit(solution)/shard_map/ppermute | solution.py:53
  46.5 5.6 %collective-permute-start.4 = (f32[7,38,128]{2,1,0:T(8,128)S(1)}, f32[7,38,128]{2,1,0:T(8,128)S(1)}, u32[]{:S(2)}, u32[]{:S(2)}) collective-permute-start(f32[7,38,128]{2,1,0:T(8,128)S(1)} %get-tuple-element.89), channel_id=1, source_target_pairs={{0,8},{8,16},{16,24},{24,32},{32,40},{40,48},{48,56},{56,64},{64,7... | collective-permute-start | bytes 408584 | tf_op jit(solution)/shard_map/ppermute | solution.py:53
  50.0 5.8 %collective-permute-start.5 = (f32[7,38,128]{2,1,0:T(8,128)S(1)}, f32[7,38,128]{2,1,0:T(8,128)S(1)}, u32[]{:S(2)}, u32[]{:S(2)}) collective-permute-start(f32[7,38,128]{2,1,0:T(8,128)S(1)} %get-tuple-element.90), channel_id=1, source_target_pairs={{8,0},{16,8},{24,16},{32,24},{40,32},{48,40},{56,48},{64,56},{72,6... | collective-permute-start | bytes 408584 | tf_op jit(solution)/shard_map/ppermute | solution.py:53
  57.3 10.0 %collective-permute-start.6 = (f32[2,3,64]{2,1,0:T(4,128)S(1)}, f32[2,3,64]{2,1,0:T(4,128)S(1)}, u32[]{:S(2)}, u32[]{:S(2)}) collective-permute-start(f32[2,3,64]{2,1,0:T(4,128)S(1)} %get-tuple-element.91), channel_id=1, source_target_pairs={{0,1},{1,2},{2,3},{3,4},{4,5},{5,6},{6,7},{8,9},{9,10},{10,11},{11... | collective-permute-start | bytes 4616 | tf_op jit(solution)/shard_map/ppermute | solution.py:53
  65.4 4.9 %collective-permute-start.7 = (f32[2,3,64]{2,1,0:T(4,128)S(1)}, f32[2,3,64]{2,1,0:T(4,128)S(1)}, u32[]{:S(2)}, u32[]{:S(2)}) collective-permute-start(f32[2,3,64]{2,1,0:T(4,128)S(1)} %get-tuple-element.92), channel_id=1, source_target_pairs={{1,0},{2,1},{3,2},{4,3},{5,4},{6,5},{7,6},{9,8},{10,9},{11,10},{12... | collective-permute-start | bytes 4616 | tf_op jit(solution)/shard_map/ppermute | solution.py:53
  70.4 5.5 %collective-permute-start.8 = (f32[3,22,64]{2,1,0:T(8,128)S(1)}, f32[3,22,64]{2,1,0:T(8,128)S(1)}, u32[]{:S(2)}, u32[]{:S(2)}) collective-permute-start(f32[3,22,64]{2,1,0:T(8,128)S(1)} %get-tuple-element.87), channel_id=1, source_target_pairs={{0,8},{8,16},{16,24},{24,32},{32,40},{40,48},{48,56},{56,64},{64,7... | collective-permute-start | bytes 50696 | tf_op jit(solution)/shard_map/ppermute | solution.py:53
  74.4 4.7 %collective-permute-start.9 = (f32[3,22,64]{2,1,0:T(8,128)S(1)}, f32[3,22,64]{2,1,0:T(8,128)S(1)}, u32[]{:S(2)}, u32[]{:S(2)}) collective-permute-start(f32[3,22,64]{2,1,0:T(8,128)S(1)} %get-tuple-element.88), channel_id=1, source_target_pairs={{8,0},{16,8},{24,16},{32,24},{40,32},{48,40},{56,48},{64,56},{72,6... | collective-permute-start | bytes 50696 | tf_op jit(solution)/shard_map/ppermute | solution.py:53
  81.2 22.0 %all-to-all-start = ((f32[128,1,512]{2,1,0:T(1,128)}), f32[128,1,512]{2,1,0:T(1,128)S(1)}, u32[]{:S(2)}, u32[]{:S(2)}) async-start(f32[128,1,512]{2,1,0:T(1,128)} %stack.2), calls=%async_computation | async-start | bytes 524288 | tf_op jit(solution)/shard_map/all_to_all | solution.py:200
